TPU v7x, 32 devices: a whole 2x2x4 slice. The times are simulated.
32 devices in a mesh: chain: 8 (over z, x), grp: 4 (over y, core).
Axes of the slice: x: 2, y: 2, z: 4, core: 2. Of those that a mesh axis runs over, the one named last changes fastest.
Arguments:
- right_side: float32 [16, 4, 64, 128], P('chain', 'grp'), may hold values from -0.8 to 0.8
- factor: float32 [16, 4, 2, 128, 128], P('chain', 'grp'), may hold values from -1 to 1
- inverse_diag: float32 [16, 4, 128, 128], P('chain', 'grp'), as said below
- pattern: int32 [16, 4, 2], P('chain'), may hold values from 0 to 3, as said below
Outputs:
- forward_result: float32 [16, 4, 64, 128], P('chain', 'grp')
- solution: float32 [16, 4, 64, 128], P('chain', 'grp')
Inputs may be any that keep to these rules, and one draw needn't show every extreme that they name: `pattern`: the 2 entries of one supernode are different supernodes of the previous level. `inverse_diag`: every block is lower triangular with a diagonal between 0.75 and 1.05.
All inputs are finite; a program needn't handle non-finite values.
Results may differ from a plain program's by a relative error of at most 0.0002.
Values sent between devices are 32-bit elements; how exact they have to be, the bound alone decides.
No kernel may reach another device: no remote copies, remote signals or barrier semaphores. Data moves between devices by JAX's collectives and lax.ppermute only.
A program may use at most 320 MiB of HBM per device.

v0:
```python
import jax
import jax.numpy as jnp
from jax import lax
from jax.sharding import PartitionSpec as P

PRECISE = lax.Precision.HIGHEST


def carried_in(value, axis, join, neutral, backward):
    count, mine = (lax.axis_size(axis), lax.axis_index(axis))
    pieces = jax.tree.map(lambda part: lax.all_gather(part, axis), value)
    if backward:
        pieces = jax.tree.map(lambda part: part[::-1], pieces)
        mine = count - 1 - mine
    subtotal = jax.tree.map(
        lambda part, zero: jnp.full_like(part, 0) + jnp.asarray(zero, part.dtype), value, neutral
    )

    def hop(position, subtotal):
        longer = join(subtotal, jax.tree.map(lambda part: part[position], pieces))
        return jax.tree.map(lambda new, old: jnp.where(position < mine, new, old), longer, subtotal)

    return lax.fori_loop(0, count - 1, hop, subtotal)


def matmul(left_side, right_factor):
    return jnp.dot(left_side, right_factor, precision=PRECISE, preferred_element_type=jnp.float32)


def matmul_trans(left_side, right_factor):
    return lax.dot_general(
        left_side,
        right_factor,
        (((1,), (1,)), ((), ())),
        precision=PRECISE,
        preferred_element_type=jnp.float32,
    )


def combine_forward(earlier_map, later_map):
    return (
        matmul(earlier_map[0], later_map[0]),
        matmul(earlier_map[1], later_map[0]) + later_map[1],
    )


def combine_backward(earlier_map, later_map):
    return (
        matmul(later_map[0], earlier_map[0]),
        matmul_trans(earlier_map[1], later_map[0]) + later_map[1],
    )


def fold_maps(running, inputs):
    return ((matmul(running[0], inputs[0]), matmul(running[1], inputs[0]) + inputs[1]), None)


def forward_step(previous, inputs):
    updated = matmul(previous, inputs[0]) + inputs[1]
    return (updated, updated)


def back_fold(running, inputs):
    return (matmul_trans(running - inputs[1], inputs[0]), None)


def shards(right_side, factor, inverse_diag, pattern):
    levels = right_side.shape[0]
    samples = right_side.shape[2]
    sup_rows = right_side.shape[3]
    groups = lax.axis_size("grp")
    level_rows = groups * sup_rows
    my_group = lax.axis_index("grp")
    scaled = jnp.einsum(
        "lgti,lgkij->lgktj",
        inverse_diag,
        factor,
        precision=PRECISE,
        preferred_element_type=jnp.float32,
    )
    lifted = jnp.einsum(
        "lgsi,lgti->lgst",
        right_side,
        inverse_diag,
        precision=PRECISE,
        preferred_element_type=jnp.float32,
    )
    blocks, offsets = (
        lax.all_gather(scaled, "grp", axis=1, tiled=True),
        lax.all_gather(lifted, "grp", axis=1, tiled=True),
    )
    onehot = (pattern[..., None] == jnp.arange(groups, dtype=jnp.int32)).astype(jnp.float32)
    level_maps = -jnp.einsum(
        "lgkh,lgktj->lhjgt", onehot, blocks, precision=PRECISE, preferred_element_type=jnp.float32
    )
    level_maps = level_maps.reshape(levels, level_rows, level_rows)
    sources = offsets.transpose(0, 2, 1, 3).reshape(levels, samples, level_rows)
    (total_map, total_shift), _ = lax.scan(
        fold_maps, (level_maps[0], sources[0]), (level_maps[1:], sources[1:])
    )
    neutral = (
        jnp.eye(level_rows, dtype=jnp.float32),
        jnp.zeros((samples, level_rows), jnp.float32),
    )
    _, incoming = carried_in((total_map, total_shift), "chain", combine_forward, neutral, False)
    _, solved = lax.scan(forward_step, incoming, (level_maps, sources))
    forward_own = lax.dynamic_slice_in_dim(solved, my_group * sup_rows, sup_rows, 2)
    back_shift, _ = lax.scan(
        back_fold, jnp.zeros((samples, level_rows), jnp.float32), (level_maps, solved), reverse=True
    )
    _, arriving = carried_in((total_map, back_shift), "chain", combine_backward, neutral, True)
    own_inverse = inverse_diag[:, 0]

    def back_step(running, inputs):
        level_map, forward_rows, inverse = inputs
        own_rows = lax.dynamic_slice_in_dim(forward_rows, my_group * sup_rows, sup_rows, 1)
        own_pending = lax.dynamic_slice_in_dim(running, my_group * sup_rows, sup_rows, 1)
        answer = matmul(own_rows - own_pending, inverse)
        return (matmul_trans(running - forward_rows, level_map), answer)

    _, answers = lax.scan(back_step, arriving, (level_maps, solved, own_inverse), reverse=True)
    return (forward_own[:, None], answers[:, None])


def solution(mesh):
    return jax.shard_map(
        shards,
        mesh=mesh,
        in_specs=(
            P("chain", "grp", None, None),
            P("chain", "grp", None, None, None),
            P("chain", "grp", None, None),
            P("chain", None, None),
        ),
        out_specs=(P("chain", "grp", None, None), P("chain", "grp", None, None)),
        check_vma=False,
    )
```

profile of v0, /device:TPU:0, one launch (start us, length us, event | category | flops | bytes accessed | tf_op | source)
XLA Modules:
  0.0 289.6 jit_solution(16148861564298682824)
XLA Ops:
  7.2 0.0 copy-start
  7.2 0.0 all-gather.9.cloned.1.call-start
  7.2 0.9 copy-done
  8.1 1.5 convolution_bitcast_fusion.4
  9.6 0.8 copy.22
  10.4 0.0 all-gather.9.cloned.1.call-update
  10.5 0.0 all-gather.13.cloned.1.call-start
  10.5 0.8 copy.23
  11.3 1.3 fusion.50
  12.6 7.2 %all-gather.1 = f32[2,256,128]{2,1,0:T(8,128)S(1)} all-gather(f32[2,64,128]{2,1,0:T(8,128)S(1)} %fusion.50), channel_id=3, replica_groups=mesh['chain'=8,'grp'=4] {'grp'}, dimensions={1}, use_global_device_ids=true | all-gather | bytes 327680 | tf_op jit(solution)/shard_map/all_gather | solution.py:90
  19.9 0.2 copy.56
  20.0 0.0 copy-start.3
  20.0 0.7 fusion.58
  20.8 0.0 copy-done.3
  20.8 9.2 %all-gather.9.cloned.1.call-done = f32[2,4,2,128,128]{4,3,2,0,1:T(8,128)} async-done(((f32[2,1,2,128,128]{4,3,2,0,1:T(8,128)}), f32[2,4,2,128,128]{4,3,2,0,1:T(8,128)}) %all-gather.9.cloned.1.call-update) | async-done | bytes 1048592 | tf_op jit(solution)/shard_map/all_gather | solution.py:89
  30.1 3.9 %negate_bitcast_fusion = f32[2,4,128,4,128]{2,1,4,3,0:T(4,128)S(1)} fusion(f32[2,4,2,128,128]{4,3,2,0,1:T(8,128)} %all-gather.9.cloned.1.call-done, s32[2,4,2]{2,1,0:T(4,128)S(1)} %copy.23), kind=kOutput, calls=%fused_computation.46 | convolution fusion | flops 13107264 | bytes 3145792 | tf_op jit(solution)/shard_map/lgkh,lgktj->lhjgt/dot_general | solution.py:93
  34.0 0.0 copy-start.4
  34.0 1.1 fusion.57
  35.1 1.8 convolution_add_fusion
  36.9 0.0 all-gather.13.cloned.1.call-update
  36.9 0.0 all-gather.11.cloned.1.call-start
  37.0 5.7 %fusion.39 = f32[512,512]{1,0:T(8,128)} fusion(f32[64,8,4,128]{3,2,1,0:T(4,128)} %bitcast.155, f32[64,8,4,128]{3,2,1,0:T(4,128)S(1)} %bitcast.154), kind=kOutput, calls=%fused_computation.50 | convolution fusion | flops 1610612736 | bytes 3145728 | tf_op jit(solution)/shard_map/while/body/eval_jaxpr/dot_general | solution.py:27
  42.7 0.0 all-gather.11.cloned.1.call-update
  42.7 0.2 all-gather.15.cloned.1.call-start
  42.9 1.1 reshape.43
  44.0 1.9 reshape.42
  45.9 1.9 copy.26
  47.8 29.5 %all-gather.13.cloned.1.call-done = f32[512,512]{1,0:T(8,128)} async-done(((f32[64,512]{1,0:T(8,128)}), f32[512,512]{1,0:T(8,128)}) %all-gather.13.cloned.1.call-update) | async-done | bytes 1048592 | tf_op jit(solution)/shard_map/all_gather | solution.py:11
  77.3 125.4 %all-gather.11.cloned.1.call-done = f32[4096,512]{1,0:T(8,128)} async-done(((f32[512,512]{1,0:T(8,128)}), f32[4096,512]{1,0:T(8,128)}) %all-gather.11.cloned.1.call-update) | async-done | bytes 8388624 | tf_op jit(solution)/shard_map/all_gather | solution.py:11
  202.7 14.4 %while.79 = (s32[]{:T(128)}, f32[64,512]{1,0:T(8,128)S(1)}, s32[]{:T(128)}, f32[8,512,512]{2,1,0:T(8,128)}, f32[8,64,512]{2,1,0:T(8,128)}, /*index=5*/s32[]{:T(128)}, s32[]{:T(128)}) while((s32[]{:T(128)}, f32[64,512]{1,0:T(8,128)S(1)}, s32[]{:T(128)}, f32[8,512,512]{2,1,0:T(8,128)}, f32[8,64,512]{2,1,0:T(8,128)}, ...), condition=%wide.region_1.2_spmd.clone, body=%wide.region_0.1_spmd.clone.sunk | while | flops 201457664 | bytes 1837671 | solution.py:23
  202.7 2.0 fusion.82
  204.8 2.0 fusion.82
  206.8 2.0 fusion.82
  208.9 2.0 fusion.82
  211.0 2.0 fusion.82
  213.0 2.0 fusion.82
  215.1 2.0 fusion.82
  217.1 1.7 while.76
  217.1 0.8 bitcast_dynamic-update-slice_fusion.2
  218.0 0.8 bitcast_dynamic-update-slice_fusion.2
  218.8 2.3 while.77
  218.8 1.1 fusion.75
  220.0 1.1 fusion.75
  221.1 0.6 copy-done.1
  221.8 0.0 all-gather.15.cloned.1.call-update
  221.8 7.6 %rev.6 = f32[8,512,512]{2,1,0:T(8,128)} reverse(f32[8,512,512]{2,1,0:T(8,128)} %get-tuple-element.945), dimensions={0} | reverse | bytes 16777216 | tf_op jit(solution)/shard_map/rev | solution.py:13
  229.4 0.6 dynamic-slice_bitcast_fusion
  230.0 30.4 %all-gather.15.cloned.1.call-done = f32[512,512]{1,0:T(8,128)} async-done(((f32[64,512]{1,0:T(8,128)}), f32[512,512]{1,0:T(8,128)}) %all-gather.15.cloned.1.call-update) | async-done | bytes 1048592 | tf_op jit(solution)/shard_map/all_gather | solution.py:11
  260.4 2.3 rev.7
  262.7 16.8 %while.80 = (s32[]{:T(128)}, f32[64,512]{1,0:T(8,128)S(1)}, s32[]{:T(128)}, f32[8,512,512]{2,1,0:T(8,128)}, f32[8,64,512]{2,1,0:T(8,128)}, /*index=5*/s32[]{:T(128)}, s32[]{:T(128)}) while((s32[]{:T(128)}, f32[64,512]{1,0:T(8,128)S(1)}, s32[]{:T(128)}, f32[8,512,512]{2,1,0:T(8,128)}, f32[8,64,512]{2,1,0:T(8,128)}, ...), condition=%wide.region_7.8_spmd.clone, body=%wide.region_6.7_spmd.clone.sunk | while | flops 201457664 | bytes 1837671 | solution.py:23
  262.7 2.4 fusion.85
  265.2 2.4 fusion.85
  267.6 2.4 fusion.85
  270.0 2.4 fusion.85
  272.4 2.4 fusion.85
  274.8 2.4 fusion.85
  277.2 2.4 fusion.85
  279.6 2.8 while.78
  279.6 0.2 fusion.79
  279.9 1.1 fusion.78
  281.0 0.2 fusion.79
  281.3 1.1 fusion.78
  282.4 0.0 copy-start.5
  282.4 0.6 copy-done.5
  (29 shorter events, 0.2 us)
Async XLA Ops:
  7.2 1.0 copy-start
  7.2 22.9 %all-gather.9.cloned.1.call-start = ((), (), s32[]{:S(2)}) async-start(), calls=%async_computation | async-start | bytes 1310720 | tf_op jit(solution)/shard_map/all_gather | solution.py:89
  10.5 66.9 %all-gather.13.cloned.1.call-start = ((), (), s32[]{:S(2)}) async-start(), calls=%async_computation.2 | async-start | bytes 1179648 | tf_op jit(solution)/shard_map/all_gather | solution.py:11
  20.0 0.8 copy-start.3
  34.0 1.2 copy-start.4
  36.9 165.8 %all-gather.11.cloned.1.call-start = ((), (), s32[]{:S(2)}) async-start(), calls=%async_computation.1 | async-start | bytes 9437184 | tf_op jit(solution)/shard_map/all_gather | solution.py:11
  42.7 217.7 %all-gather.15.cloned.1.call-start = ((), (), s32[]{:S(2)}) async-start(), calls=%async_computation.3 | async-start | bytes 1179648 | tf_op jit(solution)/shard_map/all_gather | solution.py:11
  221.1 0.6 copy-start.1
  262.7 16.9 %copy-start.2 = (f32[2,1,128,128]{3,2,1,0:T(8,128)S(1)}, f32[2,1,128,128]{3,2,1,0:T(8,128)}, u32[]{:S(2)}) copy-start(f32[2,1,128,128]{3,2,1,0:T(8,128)} %param.16) | copy-start | bytes 393220
  282.4 0.6 copy-start.5
Sparse Core Ops, SparseCore 0:
  10.6 19.4 all-gather.8
  37.0 40.2 all-gather.12
  79.5 123.1 all-gather.10
  221.9 38.4 all-gather.14
where the time goes:
time: 290 us
  waiting for transfers between devices  195 us (67%)
  matrix products  51.5 us (18%)
  local copies, waits for them, and re-layouts  21.4 us (7%)
  between operations  13.9 us (5%)
  blocking collectives  7.25 us (2%)
    all_gather x3, waiting for transfers between devices, carried_in(): pieces = jax.tree.map(lambda part: lax.all_gather(part, axis), value)  185 us
    dot_general x13, matrix products, matmul(): jnp.dot(left_side, right_factor, precision=PRECISE, preferred_element_typ...  23.7 us
    dot_general x11, matrix products, matmul_trans(): lax.dot_general(left_side, right_factor, (((1,), (1,)), ((), ())), precis...  21 us
    rev x2, local copies, waits for them, and re-layouts, carried_in(): pieces = jax.tree.map(lambda part: part[::-1], pieces)  9.88 us
    all_gather x1, waiting for transfers between devices, shards(): lax.all_gather(scaled, 'grp', axis=1, tiled=True)  9.25 us
    all_gather x1, blocking collectives, shards(): lax.all_gather(lifted, 'grp', axis=1, tiled=True)  7.25 us
  transfers between devices with their start and end apart: 4, of which 4 were waited for; matrix products, arithmetic and copies ran while one was open for 8% of the time, Pallas kernels for 0%

commit v1 on v0

v1 whole, which is shorter than its diff:
```python
import jax
import jax.numpy as jnp
from jax import lax
from jax.sharding import PartitionSpec as P

PRECISE = lax.Precision.HIGHEST


def matmul(left_side, right_factor):
    return jnp.dot(left_side, right_factor, precision=PRECISE, preferred_element_type=jnp.float32)


def matmul_trans(left_side, right_factor):
    return lax.dot_general(
        left_side,
        right_factor,
        (((1,), (1,)), ((), ())),
        precision=PRECISE,
        preferred_element_type=jnp.float32,
    )


def shards(right_side, factor, inverse_diag, pattern):
    levels = right_side.shape[0]
    samples = right_side.shape[2]
    sup_rows = right_side.shape[3]
    groups = lax.axis_size("grp")
    chain = lax.axis_size("chain")
    level_rows = groups * sup_rows
    my_group = lax.axis_index("grp")
    scaled = jnp.einsum(
        "lgti,lgkij->lgktj",
        inverse_diag,
        factor,
        precision=PRECISE,
        preferred_element_type=jnp.float32,
    )
    lifted = jnp.einsum(
        "lgsi,lgti->lgst",
        right_side,
        inverse_diag,
        precision=PRECISE,
        preferred_element_type=jnp.float32,
    )
    blocks, offsets = (
        lax.all_gather(scaled, "grp", axis=1, tiled=True),
        lax.all_gather(lifted, "grp", axis=1, tiled=True),
    )
    onehot = (pattern[..., None] == jnp.arange(groups, dtype=jnp.int32)).astype(jnp.float32)
    level_maps = -jnp.einsum(
        "lgkh,lgktj->lhjgt", onehot, blocks, precision=PRECISE, preferred_element_type=jnp.float32
    )
    level_maps = level_maps.reshape(levels, level_rows, level_rows)
    sources = offsets.transpose(0, 2, 1, 3).reshape(levels, samples, level_rows)

    def forward_levels(state):
        rows = []
        for level in range(levels):
            state = matmul(state, level_maps[level]) + sources[level]
            rows.append(state)
        return rows

    ahead = [(position, position + 1) for position in range(chain - 1)]
    behind = [(position + 1, position) for position in range(chain - 1)]

    def forward_hop(_, state):
        return lax.ppermute(forward_levels(state)[-1], "chain", ahead)

    incoming = jnp.zeros((samples, level_rows), jnp.float32)
    incoming = lax.fori_loop(0, chain - 1, forward_hop, incoming)
    solved = forward_levels(incoming)

    def backward_levels(running):
        rows = [None] * levels
        for level in reversed(range(levels)):
            rows[level] = solved[level] - running
            running = matmul_trans(-rows[level], level_maps[level])
        return rows, running

    def backward_hop(_, running):
        return lax.ppermute(backward_levels(running)[1], "chain", behind)

    arriving = jnp.zeros((samples, level_rows), jnp.float32)
    arriving = lax.fori_loop(0, chain - 1, backward_hop, arriving)
    pending_rows, _ = backward_levels(arriving)

    forward_own = []
    answers = []
    for level in range(levels):
        forward_own.append(lax.dynamic_slice_in_dim(solved[level], my_group * sup_rows, sup_rows, 1))
        own_rows = lax.dynamic_slice_in_dim(pending_rows[level], my_group * sup_rows, sup_rows, 1)
        answers.append(matmul(own_rows, inverse_diag[level, 0]))
    forward_own = jnp.stack(forward_own)
    answers = jnp.stack(answers)
    return (forward_own[:, None], answers[:, None])


def solution(mesh):
    return jax.shard_map(
        shards,
        mesh=mesh,
        in_specs=(
            P("chain", "grp", None, None),
            P("chain", "grp", None, None, None),
            P("chain", "grp", None, None),
            P("chain", None, None),
        ),
        out_specs=(P("chain", "grp", None, None), P("chain", "grp", None, None)),
        check_vma=False,
    )
```

time: 290 us -> 226 us (0.78)
  waiting for transfers between devices: 195 us -> 78.1 us
  starting transfers between devices: 0.34 us -> 41.5 us
  matrix products: 51.5 us -> 69.3 us
  local copies, waits for them, and re-layouts: 21.4 us -> 11.8 us
    all_gather x3 -> x0, waiting for transfers between devices: 185 us -> none  [carried_in(): pieces = jax.tree.map(lambda part: lax.all_gather(part, axis), value)]
    ppermute x0 -> x14, waiting for transfers between devices: none -> 70 us  [the longest x7 49.8 us: backward_hop(): return lax.ppermute(backward_levels(running)[1], 'chain', behind)]
    ppermute x0 -> x14, starting transfers between devices: none -> 41.4 us  [the longest x7 32.5 us: forward_hop(): return lax.ppermute(forward_levels(state)[-1], 'chain', ahead)]
    dot_general x13 -> x18, matrix products: 23.7 us -> 34.8 us  [matmul(): jnp.dot(left_side, right_factor, precision=PRECISE, preferred_element_typ...]
    rev x2 -> x0, local copies, waits for them, and re-layouts: 9.88 us -> none  [carried_in(): pieces = jax.tree.map(lambda part: part[::-1], pieces)]
    dot_general x11 -> x15, matrix products: 21 us -> 27.8 us  [matmul_trans(): lax.dot_general(left_side, right_factor, (((1,), (1,)), ((), ())), precis...]
  transfers between devices with their start and end apart: 4 -> 15, of which waited for: 4 -> 15; matrix products, arithmetic and copies ran while one was open for 8% -> 2% of each run, Pallas kernels for 0% -> 0%
where the time goes in v1:
time: 226 us; the launch traced here: 224 us
  waiting for transfers between devices  78.1 us (35%)
  matrix products  69.3 us (31%)
  starting transfers between devices  41.5 us (18%)
  between operations  14.1 us (6%)
  local copies, waits for them, and re-layouts  11.8 us (5%)
  blocking collectives  7.25 us (3%)
    ppermute x7, waiting for transfers between devices, backward_hop(): return lax.ppermute(backward_levels(running)[1], 'chain', behind)  49.8 us
    dot_general x18, matrix products, matmul(): jnp.dot(left_side, right_factor, precision=PRECISE, preferred_element_typ...  34.8 us
    ppermute x7, starting transfers between devices, forward_hop(): return lax.ppermute(forward_levels(state)[-1], 'chain', ahead)  32.5 us
    dot_general x15, matrix products, matmul_trans(): lax.dot_general(left_side, right_factor, (((1,), (1,)), ((), ())), precis...  27.8 us
    ppermute x7, waiting for transfers between devices, forward_hop(): return lax.ppermute(forward_levels(state)[-1], 'chain', ahead)  20.3 us
    ppermute x7, starting transfers between devices, backward_hop(): return lax.ppermute(backward_levels(running)[1], 'chain', behind)  8.96 us
    all_gather x1, waiting for transfers between devices, shards(): lax.all_gather(scaled, 'grp', axis=1, tiled=True)  8 us
    all_gather x1, blocking collectives, shards(): lax.all_gather(lifted, 'grp', axis=1, tiled=True)  7.25 us
  transfers between devices with their start and end apart: 15, of which 15 were waited for; matrix products, arithmetic and copies ran while one was open for 2% of the time, Pallas kernels for 0%

profile of v1, /device:TPU:0, one launch (start us, length us, event | category | flops | bytes accessed | tf_op | source)
XLA Modules:
  0.0 224.4 jit_solution(18291246836347683198)
XLA Ops:
  8.1 1.5 convolution_bitcast_fusion
  11.3 1.3 fusion.22
  12.6 7.3 %all-gather = f32[2,256,128]{2,1,0:T(8,128)S(1)} all-gather(f32[2,64,128]{2,1,0:T(8,128)S(1)} %fusion.22), channel_id=2, replica_groups=mesh['chain'=8,'grp'=4] {'grp'}, dimensions={1}, use_global_device_ids=true | all-gather | bytes 327680 | tf_op jit(solution)/shard_map/all_gather | solution.py:47
  22.1 8.0 %all-gather.3.cloned.1.call-done = f32[2,4,2,128,128]{4,3,2,0,1:T(8,128)} async-done(((f32[2,1,2,128,128]{4,3,2,0,1:T(8,128)}), f32[2,4,2,128,128]{4,3,2,0,1:T(8,128)}) %all-gather.3.cloned.1.call-update) | async-done | bytes 1048592 | tf_op jit(solution)/shard_map/all_gather | solution.py:46
  30.1 3.9 %negate_bitcast_fusion = f32[2,4,128,4,128]{2,1,4,3,0:T(4,128)S(1)} fusion(f32[2,4,2,128,128]{4,3,2,0,1:T(8,128)} %all-gather.3.cloned.1.call-done, s32[2,4,2]{2,1,0:T(4,128)S(1)} %copy.17), kind=kOutput, calls=%fused_computation.15 | convolution fusion | flops 13107264 | bytes 3145792 | tf_op jit(solution)/shard_map/lgkh,lgktj->lhjgt/dot_general | solution.py:50
  34.0 1.9 reshape.33
  37.0 1.9 copy.20
  38.9 80.6 %while.20 = (s32[]{:T(128)}, f32[64,512]{1,0:T(8,128)S(1)}, f32[2,512,512]{2,1,0:T(8,128)S(1)}, f32[2,64,512]{2,1,0:T(8,128)}, s32[]{:T(128)}) while((s32[]{:T(128)}, f32[64,512]{1,0:T(8,128)S(1)}, f32[2,512,512]{2,1,0:T(8,128)S(1)}, f32[2,64,512]{2,1,0:T(8,128)}, s32[]{:T(128)}) %tuple.53), condition=%wide.region_1.0_spmd, body=%wide.region_0.0_spmd.sunk | while | flops 402718720 | bytes 3407973 | solution.py:70
  38.9 1.7 convolution_add_fusion.6
  40.6 2.3 %convolution_add_fusion.7 = f32[64,512]{1,0:T(8,128)} fusion(f32[64,512]{1,0:T(8,128)S(1)} %convolution_add_fusion.6, f32[2,512,512]{2,1,0:T(8,128)S(1)} %get-tuple-element.167, f32[2,64,512]{2,1,0:T(8,128)} %get-tuple-element.168), kind=kOutput, calls=%fused_computation.clone.1 | convolution fusion | flops 201359360 | bytes 1441792 | tf_op jit(solution)/shard_map/while/body/eval_jaxpr/dot_general | solution.py:10
  42.9 3.4 %collective-permute-start = (f32[64,512]{1,0:T(8,128)}, f32[64,512]{1,0:T(8,128)S(1)}, u32[]{:S(2)}, u32[]{:S(2)}) collective-permute-start(f32[64,512]{1,0:T(8,128)} %convolution_add_fusion.7), channel_id=1, source_target_pairs={{0,4},{4,8},{8,12},{12,16},{16,20},{20,24},{24,28},{1,5},{5,9},{9,... | collective-permute-start | bytes 393224 | tf_op jit(solution)/shard_map/while/body/eval_jaxpr/ppermute | solution.py:67
  46.3 3.4 %collective-permute-done = f32[64,512]{1,0:T(8,128)S(1)} collective-permute-done((f32[64,512]{1,0:T(8,128)}, f32[64,512]{1,0:T(8,128)S(1)}, u32[]{:S(2)}, u32[]{:S(2)}) %collective-permute-start) | collective-permute-done | bytes 131104 | tf_op jit(solution)/shard_map/while/body/eval_jaxpr/ppermute | solution.py:67
  49.7 1.7 convolution_add_fusion.6
  51.4 2.3 %convolution_add_fusion.7 = f32[64,512]{1,0:T(8,128)} fusion(f32[64,512]{1,0:T(8,128)S(1)} %convolution_add_fusion.6, f32[2,512,512]{2,1,0:T(8,128)S(1)} %get-tuple-element.167, f32[2,64,512]{2,1,0:T(8,128)} %get-tuple-element.168), kind=kOutput, calls=%fused_computation.clone.1 | convolution fusion | flops 201359360 | bytes 1441792 | tf_op jit(solution)/shard_map/while/body/eval_jaxpr/dot_general | solution.py:10
  53.7 4.3 %collective-permute-start = (f32[64,512]{1,0:T(8,128)}, f32[64,512]{1,0:T(8,128)S(1)}, u32[]{:S(2)}, u32[]{:S(2)}) collective-permute-start(f32[64,512]{1,0:T(8,128)} %convolution_add_fusion.7), channel_id=1, source_target_pairs={{0,4},{4,8},{8,12},{12,16},{16,20},{20,24},{24,28},{1,5},{5,9},{9,... | collective-permute-start | bytes 393224 | tf_op jit(solution)/shard_map/while/body/eval_jaxpr/ppermute | solution.py:67
  57.9 2.8 %collective-permute-done = f32[64,512]{1,0:T(8,128)S(1)} collective-permute-done((f32[64,512]{1,0:T(8,128)}, f32[64,512]{1,0:T(8,128)S(1)}, u32[]{:S(2)}, u32[]{:S(2)}) %collective-permute-start) | collective-permute-done | bytes 131104 | tf_op jit(solution)/shard_map/while/body/eval_jaxpr/ppermute | solution.py:67
  60.8 1.7 convolution_add_fusion.6
  62.4 2.3 %convolution_add_fusion.7 = f32[64,512]{1,0:T(8,128)} fusion(f32[64,512]{1,0:T(8,128)S(1)} %convolution_add_fusion.6, f32[2,512,512]{2,1,0:T(8,128)S(1)} %get-tuple-element.167, f32[2,64,512]{2,1,0:T(8,128)} %get-tuple-element.168), kind=kOutput, calls=%fused_computation.clone.1 | convolution fusion | flops 201359360 | bytes 1441792 | tf_op jit(solution)/shard_map/while/body/eval_jaxpr/dot_general | solution.py:10
  64.7 4.3 %collective-permute-start = (f32[64,512]{1,0:T(8,128)}, f32[64,512]{1,0:T(8,128)S(1)}, u32[]{:S(2)}, u32[]{:S(2)}) collective-permute-start(f32[64,512]{1,0:T(8,128)} %convolution_add_fusion.7), channel_id=1, source_target_pairs={{0,4},{4,8},{8,12},{12,16},{16,20},{20,24},{24,28},{1,5},{5,9},{9,... | collective-permute-start | bytes 393224 | tf_op jit(solution)/shard_map/while/body/eval_jaxpr/ppermute | solution.py:67
  69.0 2.8 %collective-permute-done = f32[64,512]{1,0:T(8,128)S(1)} collective-permute-done((f32[64,512]{1,0:T(8,128)}, f32[64,512]{1,0:T(8,128)S(1)}, u32[]{:S(2)}, u32[]{:S(2)}) %collective-permute-start) | collective-permute-done | bytes 131104 | tf_op jit(solution)/shard_map/while/body/eval_jaxpr/ppermute | solution.py:67
  71.8 1.7 convolution_add_fusion.6
  73.5 2.3 %convolution_add_fusion.7 = f32[64,512]{1,0:T(8,128)} fusion(f32[64,512]{1,0:T(8,128)S(1)} %convolution_add_fusion.6, f32[2,512,512]{2,1,0:T(8,128)S(1)} %get-tuple-element.167, f32[2,64,512]{2,1,0:T(8,128)} %get-tuple-element.168), kind=kOutput, calls=%fused_computation.clone.1 | convolution fusion | flops 201359360 | bytes 1441792 | tf_op jit(solution)/shard_map/while/body/eval_jaxpr/dot_general | solution.py:10
  75.8 5.1 %collective-permute-start = (f32[64,512]{1,0:T(8,128)}, f32[64,512]{1,0:T(8,128)S(1)}, u32[]{:S(2)}, u32[]{:S(2)}) collective-permute-start(f32[64,512]{1,0:T(8,128)} %convolution_add_fusion.7), channel_id=1, source_target_pairs={{0,4},{4,8},{8,12},{12,16},{16,20},{20,24},{24,28},{1,5},{5,9},{9,... | collective-permute-start | bytes 393224 | tf_op jit(solution)/shard_map/while/body/eval_jaxpr/ppermute | solution.py:67
  80.9 2.8 %collective-permute-done = f32[64,512]{1,0:T(8,128)S(1)} collective-permute-done((f32[64,512]{1,0:T(8,128)}, f32[64,512]{1,0:T(8,128)S(1)}, u32[]{:S(2)}, u32[]{:S(2)}) %collective-permute-start) | collective-permute-done | bytes 131104 | tf_op jit(solution)/shard_map/while/body/eval_jaxpr/ppermute | solution.py:67
  83.7 1.7 convolution_add_fusion.6
  85.4 2.3 %convolution_add_fusion.7 = f32[64,512]{1,0:T(8,128)} fusion(f32[64,512]{1,0:T(8,128)S(1)} %convolution_add_fusion.6, f32[2,512,512]{2,1,0:T(8,128)S(1)} %get-tuple-element.167, f32[2,64,512]{2,1,0:T(8,128)} %get-tuple-element.168), kind=kOutput, calls=%fused_computation.clone.1 | convolution fusion | flops 201359360 | bytes 1441792 | tf_op jit(solution)/shard_map/while/body/eval_jaxpr/dot_general | solution.py:10
  87.7 5.1 %collective-permute-start = (f32[64,512]{1,0:T(8,128)}, f32[64,512]{1,0:T(8,128)S(1)}, u32[]{:S(2)}, u32[]{:S(2)}) collective-permute-start(f32[64,512]{1,0:T(8,128)} %convolution_add_fusion.7), channel_id=1, source_target_pairs={{0,4},{4,8},{8,12},{12,16},{16,20},{20,24},{24,28},{1,5},{5,9},{9,... | collective-permute-start | bytes 393224 | tf_op jit(solution)/shard_map/while/body/eval_jaxpr/ppermute | solution.py:67
  92.8 2.8 %collective-permute-done = f32[64,512]{1,0:T(8,128)S(1)} collective-permute-done((f32[64,512]{1,0:T(8,128)}, f32[64,512]{1,0:T(8,128)S(1)}, u32[]{:S(2)}, u32[]{:S(2)}) %collective-permute-start) | collective-permute-done | bytes 131104 | tf_op jit(solution)/shard_map/while/body/eval_jaxpr/ppermute | solution.py:67
  95.7 1.7 convolution_add_fusion.6
  97.3 2.3 %convolution_add_fusion.7 = f32[64,512]{1,0:T(8,128)} fusion(f32[64,512]{1,0:T(8,128)S(1)} %convolution_add_fusion.6, f32[2,512,512]{2,1,0:T(8,128)S(1)} %get-tuple-element.167, f32[2,64,512]{2,1,0:T(8,128)} %get-tuple-element.168), kind=kOutput, calls=%fused_computation.clone.1 | convolution fusion | flops 201359360 | bytes 1441792 | tf_op jit(solution)/shard_map/while/body/eval_jaxpr/dot_general | solution.py:10
  99.6 5.1 %collective-permute-start = (f32[64,512]{1,0:T(8,128)}, f32[64,512]{1,0:T(8,128)S(1)}, u32[]{:S(2)}, u32[]{:S(2)}) collective-permute-start(f32[64,512]{1,0:T(8,128)} %convolution_add_fusion.7), channel_id=1, source_target_pairs={{0,4},{4,8},{8,12},{12,16},{16,20},{20,24},{24,28},{1,5},{5,9},{9,... | collective-permute-start | bytes 393224 | tf_op jit(solution)/shard_map/while/body/eval_jaxpr/ppermute | solution.py:67
  104.8 2.8 %collective-permute-done = f32[64,512]{1,0:T(8,128)S(1)} collective-permute-done((f32[64,512]{1,0:T(8,128)}, f32[64,512]{1,0:T(8,128)S(1)}, u32[]{:S(2)}, u32[]{:S(2)}) %collective-permute-start) | collective-permute-done | bytes 131104 | tf_op jit(solution)/shard_map/while/body/eval_jaxpr/ppermute | solution.py:67
  107.6 1.7 convolution_add_fusion.6
  109.2 2.3 %convolution_add_fusion.7 = f32[64,512]{1,0:T(8,128)} fusion(f32[64,512]{1,0:T(8,128)S(1)} %convolution_add_fusion.6, f32[2,512,512]{2,1,0:T(8,128)S(1)} %get-tuple-element.167, f32[2,64,512]{2,1,0:T(8,128)} %get-tuple-element.168), kind=kOutput, calls=%fused_computation.clone.1 | convolution fusion | flops 201359360 | bytes 1441792 | tf_op jit(solution)/shard_map/while/body/eval_jaxpr/dot_general | solution.py:10
  111.5 5.1 %collective-permute-start = (f32[64,512]{1,0:T(8,128)}, f32[64,512]{1,0:T(8,128)S(1)}, u32[]{:S(2)}, u32[]{:S(2)}) collective-permute-start(f32[64,512]{1,0:T(8,128)} %convolution_add_fusion.7), channel_id=1, source_target_pairs={{0,4},{4,8},{8,12},{12,16},{16,20},{20,24},{24,28},{1,5},{5,9},{9,... | collective-permute-start | bytes 393224 | tf_op jit(solution)/shard_map/while/body/eval_jaxpr/ppermute | solution.py:67
  116.7 2.8 %collective-permute-done = f32[64,512]{1,0:T(8,128)S(1)} collective-permute-done((f32[64,512]{1,0:T(8,128)}, f32[64,512]{1,0:T(8,128)S(1)}, u32[]{:S(2)}, u32[]{:S(2)}) %collective-permute-start) | collective-permute-done | bytes 131104 | tf_op jit(solution)/shard_map/while/body/eval_jaxpr/ppermute | solution.py:67
  120.1 2.4 %convolution_add_fusion.3 = f32[64,512]{1,0:T(8,128)S(1)} fusion(f32[64,512]{1,0:T(8,128)} %copy-done.1, f32[64,8,4,128]{3,2,1,0:T(4,128)} %bitcast.120, f32[8,8,4,128]{3,2,1,0:T(4,128)} %bitcast.124), kind=kOutput, calls=%fused_computation.18 | convolution fusion | flops 201359360 | bytes 1441792 | tf_op jit(solution)/shard_map/dot_general | solution.py:10
  122.5 2.7 %convolution_add_fusion.2 = f32[64,512]{1,0:T(8,128)} fusion(f32[64,512]{1,0:T(8,128)S(1)} %convolution_add_fusion.3, f32[64,8,4,128]{3,2,1,0:T(4,128)S(1)} %bitcast.117, f32[8,8,4,128]{3,2,1,0:T(4,128)} %bitcast.123), kind=kOutput, calls=%fused_computation.17 | convolution fusion | flops 201359360 | bytes 1441792 | tf_op jit(solution)/shard_map/dot_general | solution.py:10
  125.8 85.9 %while.21 = (s32[]{:T(128)}, f32[64,512]{1,0:T(8,128)}, f32[64,512]{1,0:T(8,128)}, f32[2,512,512]{2,1,0:T(8,128)S(1)}, f32[64,512]{1,0:T(8,128)S(1)}, /*index=5*/s32[]{:T(128)}) while((s32[]{:T(128)}, f32[64,512]{1,0:T(8,128)}, f32[64,512]{1,0:T(8,128)}, f32[2,512,512]{2,1,0:T(8,128)S(1)}, f32[64,512]{1,0:T(8,128)S(1)}, ...), condition=%wide.region_3.0_spmd, body=%wide.region_2.0_spmd.sunk | while | flops 402784256 | bytes 3407981 | solution.py:84
  125.8 2.1 fusion.63
  127.9 1.8 fusion.64
  129.7 1.3 collective-permute-start.1
  131.0 7.1 %collective-permute-done.1 = f32[64,512]{1,0:T(8,128)} collective-permute-done((f32[64,512]{1,0:T(8,128)}, f32[64,512]{1,0:T(8,128)}, u32[]{:S(2)}, u32[]{:S(2)}) %collective-permute-start.1) | collective-permute-done | bytes 131104 | tf_op jit(solution)/shard_map/while/body/eval_jaxpr/ppermute | solution.py:81
  138.1 2.1 fusion.63
  140.2 1.8 fusion.64
  142.0 1.3 collective-permute-start.1
  143.2 7.1 %collective-permute-done.1 = f32[64,512]{1,0:T(8,128)} collective-permute-done((f32[64,512]{1,0:T(8,128)}, f32[64,512]{1,0:T(8,128)}, u32[]{:S(2)}, u32[]{:S(2)}) %collective-permute-start.1) | collective-permute-done | bytes 131104 | tf_op jit(solution)/shard_map/while/body/eval_jaxpr/ppermute | solution.py:81
  150.3 2.1 fusion.63
  152.4 1.8 fusion.64
  154.2 1.3 collective-permute-start.1
  155.5 7.6 %collective-permute-done.1 = f32[64,512]{1,0:T(8,128)} collective-permute-done((f32[64,512]{1,0:T(8,128)}, f32[64,512]{1,0:T(8,128)}, u32[]{:S(2)}, u32[]{:S(2)}) %collective-permute-start.1) | collective-permute-done | bytes 131104 | tf_op jit(solution)/shard_map/while/body/eval_jaxpr/ppermute | solution.py:81
  163.1 2.1 fusion.63
  165.2 1.8 fusion.64
  167.0 1.3 collective-permute-start.1
  168.3 7.9 %collective-permute-done.1 = f32[64,512]{1,0:T(8,128)} collective-permute-done((f32[64,512]{1,0:T(8,128)}, f32[64,512]{1,0:T(8,128)}, u32[]{:S(2)}, u32[]{:S(2)}) %collective-permute-start.1) | collective-permute-done | bytes 131104 | tf_op jit(solution)/shard_map/while/body/eval_jaxpr/ppermute | solution.py:81
  176.2 2.1 fusion.63
  178.3 1.8 fusion.64
  181.3 6.5 %collective-permute-done.1 = f32[64,512]{1,0:T(8,128)} collective-permute-done((f32[64,512]{1,0:T(8,128)}, f32[64,512]{1,0:T(8,128)}, u32[]{:S(2)}, u32[]{:S(2)}) %collective-permute-start.1) | collective-permute-done | bytes 131104 | tf_op jit(solution)/shard_map/while/body/eval_jaxpr/ppermute | solution.py:81
  187.8 2.1 fusion.63
  189.9 1.8 fusion.64
  193.0 6.8 %collective-permute-done.1 = f32[64,512]{1,0:T(8,128)} collective-permute-done((f32[64,512]{1,0:T(8,128)}, f32[64,512]{1,0:T(8,128)}, u32[]{:S(2)}, u32[]{:S(2)}) %collective-permute-start.1) | collective-permute-done | bytes 131104 | tf_op jit(solution)/shard_map/while/body/eval_jaxpr/ppermute | solution.py:81
  199.8 2.1 fusion.63
  201.9 1.8 fusion.64
  204.9 6.8 %collective-permute-done.1 = f32[64,512]{1,0:T(8,128)} collective-permute-done((f32[64,512]{1,0:T(8,128)}, f32[64,512]{1,0:T(8,128)}, u32[]{:S(2)}, u32[]{:S(2)}) %collective-permute-start.1) | collective-permute-done | bytes 131104 | tf_op jit(solution)/shard_map/while/body/eval_jaxpr/ppermute | solution.py:81
  (25 shorter events, 16.9 us)
Async XLA Ops:
  7.2 1.0 copy-start
  7.2 22.9 %all-gather.3.cloned.1.call-start = ((), (), s32[]{:S(2)}) async-start(), calls=%async_computation | async-start | bytes 1310720 | tf_op jit(solution)/shard_map/all_gather | solution.py:46
  42.9 6.8 %collective-permute-start = (f32[64,512]{1,0:T(8,128)}, f32[64,512]{1,0:T(8,128)S(1)}, u32[]{:S(2)}, u32[]{:S(2)}) collective-permute-start(f32[64,512]{1,0:T(8,128)} %convolution_add_fusion.7), channel_id=1, source_target_pairs={{0,4},{4,8},{8,12},{12,16},{16,20},{20,24},{24,28},{1,5},{5,9},{9,... | collective-permute-start | bytes 393224 | tf_op jit(solution)/shard_map/while/body/eval_jaxpr/ppermute | solution.py:67
  53.7 7.1 %collective-permute-start = (f32[64,512]{1,0:T(8,128)}, f32[64,512]{1,0:T(8,128)S(1)}, u32[]{:S(2)}, u32[]{:S(2)}) collective-permute-start(f32[64,512]{1,0:T(8,128)} %convolution_add_fusion.7), channel_id=1, source_target_pairs={{0,4},{4,8},{8,12},{12,16},{16,20},{20,24},{24,28},{1,5},{5,9},{9,... | collective-permute-start | bytes 393224 | tf_op jit(solution)/shard_map/while/body/eval_jaxpr/ppermute | solution.py:67
  64.7 7.1 %collective-permute-start = (f32[64,512]{1,0:T(8,128)}, f32[64,512]{1,0:T(8,128)S(1)}, u32[]{:S(2)}, u32[]{:S(2)}) collective-permute-start(f32[64,512]{1,0:T(8,128)} %convolution_add_fusion.7), channel_id=1, source_target_pairs={{0,4},{4,8},{8,12},{12,16},{16,20},{20,24},{24,28},{1,5},{5,9},{9,... | collective-permute-start | bytes 393224 | tf_op jit(solution)/shard_map/while/body/eval_jaxpr/ppermute | solution.py:67
  75.8 8.0 %collective-permute-start = (f32[64,512]{1,0:T(8,128)}, f32[64,512]{1,0:T(8,128)S(1)}, u32[]{:S(2)}, u32[]{:S(2)}) collective-permute-start(f32[64,512]{1,0:T(8,128)} %convolution_add_fusion.7), channel_id=1, source_target_pairs={{0,4},{4,8},{8,12},{12,16},{16,20},{20,24},{24,28},{1,5},{5,9},{9,... | collective-permute-start | bytes 393224 | tf_op jit(solution)/shard_map/while/body/eval_jaxpr/ppermute | solution.py:67
  87.7 8.0 %collective-permute-start = (f32[64,512]{1,0:T(8,128)}, f32[64,512]{1,0:T(8,128)S(1)}, u32[]{:S(2)}, u32[]{:S(2)}) collective-permute-start(f32[64,512]{1,0:T(8,128)} %convolution_add_fusion.7), channel_id=1, source_target_pairs={{0,4},{4,8},{8,12},{12,16},{16,20},{20,24},{24,28},{1,5},{5,9},{9,... | collective-permute-start | bytes 393224 | tf_op jit(solution)/shard_map/while/body/eval_jaxpr/ppermute | solution.py:67
  99.6 8.0 %collective-permute-start = (f32[64,512]{1,0:T(8,128)}, f32[64,512]{1,0:T(8,128)S(1)}, u32[]{:S(2)}, u32[]{:S(2)}) collective-permute-start(f32[64,512]{1,0:T(8,128)} %convolution_add_fusion.7), channel_id=1, source_target_pairs={{0,4},{4,8},{8,12},{12,16},{16,20},{20,24},{24,28},{1,5},{5,9},{9,... | collective-permute-start | bytes 393224 | tf_op jit(solution)/shard_map/while/body/eval_jaxpr/ppermute | solution.py:67
  111.5 8.0 %collective-permute-start = (f32[64,512]{1,0:T(8,128)}, f32[64,512]{1,0:T(8,128)S(1)}, u32[]{:S(2)}, u32[]{:S(2)}) collective-permute-start(f32[64,512]{1,0:T(8,128)} %convolution_add_fusion.7), channel_id=1, source_target_pairs={{0,4},{4,8},{8,12},{12,16},{16,20},{20,24},{24,28},{1,5},{5,9},{9,... | collective-permute-start | bytes 393224 | tf_op jit(solution)/shard_map/while/body/eval_jaxpr/ppermute | solution.py:67
  119.5 0.6 copy-start.1
  129.7 8.4 %collective-permute-start.1 = (f32[64,512]{1,0:T(8,128)}, f32[64,512]{1,0:T(8,128)}, u32[]{:S(2)}, u32[]{:S(2)}) collective-permute-start(f32[64,512]{1,0:T(8,128)} %fusion.64), channel_id=1, source_target_pairs={{4,0},{8,4},{12,8},{16,12},{20,16},{24,20},{28,24},{5,1},{9,5},{13... | collective-permute-start | bytes 393224 | tf_op jit(solution)/shard_map/while/body/eval_jaxpr/ppermute | solution.py:81
  142.0 8.4 %collective-permute-start.1 = (f32[64,512]{1,0:T(8,128)}, f32[64,512]{1,0:T(8,128)}, u32[]{:S(2)}, u32[]{:S(2)}) collective-permute-start(f32[64,512]{1,0:T(8,128)} %fusion.64), channel_id=1, source_target_pairs={{4,0},{8,4},{12,8},{16,12},{20,16},{24,20},{28,24},{5,1},{9,5},{13... | collective-permute-start | bytes 393224 | tf_op jit(solution)/shard_map/while/body/eval_jaxpr/ppermute | solution.py:81
  154.2 8.9 %collective-permute-start.1 = (f32[64,512]{1,0:T(8,128)}, f32[64,512]{1,0:T(8,128)}, u32[]{:S(2)}, u32[]{:S(2)}) collective-permute-start(f32[64,512]{1,0:T(8,128)} %fusion.64), channel_id=1, source_target_pairs={{4,0},{8,4},{12,8},{16,12},{20,16},{24,20},{28,24},{5,1},{9,5},{13... | collective-permute-start | bytes 393224 | tf_op jit(solution)/shard_map/while/body/eval_jaxpr/ppermute | solution.py:81
  167.0 9.2 %collective-permute-start.1 = (f32[64,512]{1,0:T(8,128)}, f32[64,512]{1,0:T(8,128)}, u32[]{:S(2)}, u32[]{:S(2)}) collective-permute-start(f32[64,512]{1,0:T(8,128)} %fusion.64), channel_id=1, source_target_pairs={{4,0},{8,4},{12,8},{16,12},{20,16},{24,20},{28,24},{5,1},{9,5},{13... | collective-permute-start | bytes 393224 | tf_op jit(solution)/shard_map/while/body/eval_jaxpr/ppermute | solution.py:81
  180.1 7.8 %collective-permute-start.1 = (f32[64,512]{1,0:T(8,128)}, f32[64,512]{1,0:T(8,128)}, u32[]{:S(2)}, u32[]{:S(2)}) collective-permute-start(f32[64,512]{1,0:T(8,128)} %fusion.64), channel_id=1, source_target_pairs={{4,0},{8,4},{12,8},{16,12},{20,16},{24,20},{28,24},{5,1},{9,5},{13... | collective-permute-start | bytes 393224 | tf_op jit(solution)/shard_map/while/body/eval_jaxpr/ppermute | solution.py:81
  191.7 8.1 %collective-permute-start.1 = (f32[64,512]{1,0:T(8,128)}, f32[64,512]{1,0:T(8,128)}, u32[]{:S(2)}, u32[]{:S(2)}) collective-permute-start(f32[64,512]{1,0:T(8,128)} %fusion.64), channel_id=1, source_target_pairs={{4,0},{8,4},{12,8},{16,12},{20,16},{24,20},{28,24},{5,1},{9,5},{13... | collective-permute-start | bytes 393224 | tf_op jit(solution)/shard_map/while/body/eval_jaxpr/ppermute | solution.py:81
  203.6 8.1 %collective-permute-start.1 = (f32[64,512]{1,0:T(8,128)}, f32[64,512]{1,0:T(8,128)}, u32[]{:S(2)}, u32[]{:S(2)}) collective-permute-start(f32[64,512]{1,0:T(8,128)} %fusion.64), channel_id=1, source_target_pairs={{4,0},{8,4},{12,8},{16,12},{20,16},{24,20},{28,24},{5,1},{9,5},{13... | collective-permute-start | bytes 393224 | tf_op jit(solution)/shard_map/while/body/eval_jaxpr/ppermute | solution.py:81
Sparse Core Ops, SparseCore 0:
  10.6 19.4 all-gather.2
